TPU v7x, 32 devices: a whole 2x2x4 slice. The times are simulated.
32 devices in a mesh: ctx: 4 (over y, x), pair: 4 (over z), dp: 2 (over core).
Axes of the slice: x: 2, y: 2, z: 4, core: 2. Of those that a mesh axis runs over, the one named last changes fastest.
Arguments:
- queries: bfloat16 [8, 4, 128, 2048], P(('dp', 'ctx'), 'pair'), parts along dimension 0, may hold values from -8 to 8
- resp_keys: bfloat16 [8, 4, 128, 1024], P(('dp', 'ctx'), 'pair'), parts along dimension 0, may hold values from -6 to 6
- resp_values: bfloat16 [8, 4, 128, 1024], P(('dp', 'ctx'), 'pair'), parts along dimension 0, may hold values from -6 to 6
- d_out: bfloat16 [8, 4, 128, 2048], P(('dp', 'ctx'), 'pair'), parts along dimension 0, may hold values from -6 to 6
- prefix_kv: bfloat16 [4, 512, 2, 1024], P('dp', 'ctx', None, 'pair'), parts along dimension 0, may hold values from -8 to 8
- prefix_blocks: int32 [8, 4, 4], P(('dp', 'ctx'), 'pair'), parts along dimension 0, may hold values 0 or 1
- resp_lengths: int32 [8, 4], P(('dp', 'ctx'), 'pair'), parts along dimension 0, may hold values from 32 to 128, as said below
- pair_prompt: int32 [8], P('dp'), parts along dimension 0, may hold values from 0 to 1, as said below
Outputs:
- d_queries: bfloat16 [8, 4, 128, 2048], P(('dp', 'ctx'), 'pair'), parts along dimension 0
- d_resp_keys: bfloat16 [8, 4, 128, 1024], P(('dp', 'ctx'), 'pair'), parts along dimension 0
- d_resp_values: bfloat16 [8, 4, 128, 1024], P(('dp', 'ctx'), 'pair'), parts along dimension 0
- d_prefix: float32 [4, 512, 2, 1024], P('dp', 'ctx', None, 'pair'), parts along dimension 0
There are 2 independent parts, one for each index of `dp`. A program takes and returns all parts, laid end to end along the dimension named above; each array names one. Nothing has to cross between parts.
Inputs may be any that keep to these rules, and one draw needn't show every extreme that they name: `pair_prompt`: each prompt is answered by exactly two indices of pair, one chosen and one rejected response. `resp_lengths`: some response fills all 128 slots.
All inputs are finite; a program needn't handle non-finite values. No bound on the sum of `prefix_blocks` on one device may be relied on, other than what follows from the above.
Results may differ from a plain program's by a relative error of at most 0.012.
The roundings to bfloat16 on the way count: a program that leaves them out, or rounds other values in their place, can miss the bound.
Values may be sent and summed in bfloat16 or wider, within the bound.
No kernel may reach another device: no remote copies, remote signals or barrier semaphores. Data moves between devices by JAX's collectives and lax.ppermute only.
A program may use at most 128 MiB of HBM per device.

v0:
```python
import jax
import jax.numpy as jnp
from jax import lax
from jax.sharding import PartitionSpec as P

KV_HEADS = 8
GROUP = 2
HEAD_DIM = 128
BLOCK = 128
scale_factor = 144.0 ** (-0.5)
neg_big = -1e30


def gather_rows(kv_part):
    return lax.all_gather(kv_part, "ctx", axis=1, tiled=True)


def pick_prompt(kv_part, pair_prompt):
    outgoing = jnp.take(kv_part, pair_prompt, axis=0)
    return lax.all_to_all(outgoing, "pair", split_axis=0, concat_axis=3, tiled=True)


def shards(
    queries, resp_keys, resp_values, d_out, prefix_kv, prefix_blocks, resp_lengths, pair_prompt
):
    prefix_panel = gather_rows(pick_prompt(prefix_kv, pair_prompt))
    prefix_panel = prefix_panel[0]
    resp_rows = queries.shape[2]
    pre_rows = prefix_panel.shape[0]
    n_prompts = prefix_kv.shape[0]
    all_rows = pre_rows + resp_rows
    keys_heads = jnp.transpose(
        jnp.concatenate([prefix_panel[:, 0], resp_keys[0, 0]], 0).reshape(
            all_rows, KV_HEADS, HEAD_DIM
        ),
        (1, 0, 2),
    )
    values_heads = jnp.transpose(
        jnp.concatenate([prefix_panel[:, 1], resp_values[0, 0]], 0).reshape(
            all_rows, KV_HEADS, HEAD_DIM
        ),
        (1, 0, 2),
    )
    query_heads = jnp.transpose(
        queries[0, 0].reshape(resp_rows, KV_HEADS, GROUP, HEAD_DIM), (1, 2, 0, 3)
    )
    positions = jnp.arange(resp_rows, dtype=jnp.int32)
    live_rows = positions < resp_lengths[0, 0]
    grad_rows = jnp.where(live_rows[:, None], d_out[0, 0], jnp.zeros_like(d_out[0, 0]))
    grad_heads = jnp.transpose(
        grad_rows.reshape(resp_rows, KV_HEADS, GROUP, HEAD_DIM), (1, 2, 0, 3)
    )
    visible = prefix_blocks[0, 0] > 0
    prefix_mask = jnp.broadcast_to(visible[:, None], (pre_rows // BLOCK, BLOCK)).reshape(pre_rows)
    causal = positions[:, None] >= positions[None, :]
    allowed = jnp.concatenate(
        [jnp.broadcast_to(prefix_mask[None, :], (resp_rows, pre_rows)), causal], 1
    )

    def one_head(items):
        key_rows, value_rows, query_rows, grad_part = items
        scores = (
            jnp.einsum("jqd,kd->jqk", query_rows, key_rows, preferred_element_type=jnp.float32)
            * scale_factor
        )
        scores = jnp.where(allowed[None], scores, neg_big)
        row_peak = jnp.max(scores, axis=-1, keepdims=True)
        raised = jnp.exp(scores - row_peak)
        weights = raised / jnp.sum(raised, axis=-1, keepdims=True)
        probs_low = weights.astype(jnp.bfloat16)
        attended = jnp.einsum(
            "jqk,kd->jqd", probs_low, value_rows, preferred_element_type=jnp.float32
        )
        attended = lax.optimization_barrier(attended.astype(jnp.bfloat16)).astype(jnp.float32)
        row_delta = jnp.sum(grad_part.astype(jnp.float32) * attended, axis=-1)
        d_probs = jnp.einsum(
            "jqd,kd->jqk", grad_part, value_rows, preferred_element_type=jnp.float32
        )
        ds_low = (weights * (d_probs - row_delta[..., None])).astype(jnp.bfloat16)
        query_grad = (
            jnp.einsum("jqk,kd->jqd", ds_low, key_rows, preferred_element_type=jnp.float32)
            * scale_factor
        )
        key_grad = (
            jnp.einsum("jqk,jqd->kd", ds_low, query_rows, preferred_element_type=jnp.float32)
            * scale_factor
        )
        value_grad = jnp.einsum(
            "jqk,jqd->kd", probs_low, grad_part, preferred_element_type=jnp.float32
        )
        both_grads = jnp.stack([key_grad, value_grad], 1).astype(jnp.bfloat16)
        return (query_grad.astype(jnp.bfloat16), both_grads)

    query_grads, kv_grads = lax.map(one_head, (keys_heads, values_heads, query_heads, grad_heads))
    d_queries = jnp.transpose(query_grads, (2, 0, 1, 3)).reshape(1, 1, resp_rows, -1)
    own_grads = jnp.transpose(kv_grads[:, pre_rows:], (1, 2, 0, 3)).reshape(resp_rows, 2, -1)
    d_resp_keys = own_grads[:, 0].reshape(1, 1, resp_rows, -1)
    d_resp_values = own_grads[:, 1].reshape(1, 1, resp_rows, -1)
    prefix_part = jnp.transpose(kv_grads[:, :pre_rows], (1, 2, 0, 3)).reshape(1, pre_rows, 2, -1)
    pieces = lax.all_to_all(prefix_part, "ctx", split_axis=1, concat_axis=0, tiled=True)
    ctx_total = jnp.sum(pieces.astype(jnp.float32), axis=0).astype(jnp.bfloat16)
    arrived = lax.all_to_all(ctx_total[None], "pair", split_axis=3, concat_axis=0, tiled=True)
    prompt_hits = (pair_prompt[:, None] == jnp.arange(n_prompts, dtype=jnp.int32)[None, :]).astype(
        jnp.float32
    )
    d_prefix = jnp.sum(
        prompt_hits[:, :, None, None, None] * arrived.astype(jnp.float32)[:, None], axis=0
    )
    return (d_queries, d_resp_keys, d_resp_values, d_prefix)


def solution(mesh):
    placed = (
        P(("dp", "ctx"), "pair", None, None),
        P(("dp", "ctx"), "pair", None, None),
        P(("dp", "ctx"), "pair", None, None),
        P(("dp", "ctx"), "pair", None, None),
        P("dp", "ctx", None, "pair"),
        P(("dp", "ctx"), "pair", None),
        P(("dp", "ctx"), "pair"),
        P("dp"),
    )
    return jax.shard_map(
        shards,
        mesh=mesh,
        in_specs=placed,
        out_specs=(
            P(("dp", "ctx"), "pair", None, None),
            P(("dp", "ctx"), "pair", None, None),
            P(("dp", "ctx"), "pair", None, None),
            P("dp", "ctx", None, "pair"),
        ),
        check_vma=False,
    )
```

profile of v0, /device:TPU:0, one launch (start us, length us, event | category | flops | bytes accessed | tf_op | source)
XLA Modules:
  0.0 192.6 jit_solution(804473975615161115)
XLA Ops:
  8.6 1.6 gather_fusion
  10.8 20.7 %all_to_all.39 = bf16[4,128,2,256]{3,2,1,0:T(2,128)(2,1)S(1)} all-to-all(bf16[4,128,2,256]{3,2,1,0:T(2,128)(2,1)S(1)} %broadcast_select_fusion), channel_id=1, replica_groups=mesh['ctx'=4,'pair'=4,'dp'=2] {'pair'}, dimensions={0} | all-to-all | bytes 1048576 | tf_op jit(solution)/shard_map/all_to_all | solution.py:20
  35.3 31.8 %all-gather.2.cloned.1.call-done = bf16[1,512,2,1024]{1,3,2,0:T(8,128)(2,1)} async-done(((bf16[1,128,2,1024]{1,3,2,0:T(8,128)(2,1)}), bf16[1,512,2,1024]{1,3,2,0:T(8,128)(2,1)}) %all-gather.2.cloned.1.call-update) | async-done | bytes 2097168 | tf_op jit(solution)/shard_map/all_gather | solution.py:15
  67.1 1.7 fusion.55
  68.7 1.3 maximum_bitcast_fusion
  70.1 50.9 %while.12 = (s32[]{:T(128)}, bf16[8,2,128,128]{3,2,1,0:T(8,128)(2,1)}, bf16[8,640,2,128]{3,1,2,0:T(8,128)(2,1)}, pred[128,640]{1,0:T(8,128)(4,1)S(1)}, bf16[8,2,...) while((s32[]{:T(128)}, ...), condition=%wide.region_4.5_spmd, body=%wide.region_0.4_spmd.sunk | while | flops 254427520 | bytes 6446201 | solution.py:94
  70.1 1.4 fusion.90
  73.3 1.8 fusion.93
  76.4 1.4 fusion.90
  79.6 1.8 fusion.93
  82.8 1.4 fusion.90
  86.0 1.8 fusion.93
  89.1 1.4 fusion.90
  92.4 1.8 fusion.93
  95.5 1.4 fusion.90
  98.7 1.8 fusion.93
  101.9 1.4 fusion.90
  105.1 1.8 fusion.93
  108.2 1.4 fusion.90
  111.4 1.8 fusion.93
  114.6 1.4 fusion.90
  117.8 1.8 fusion.93
  121.0 3.2 %copy.93 = bf16[8,640,2,128]{1,3,0,2:T(8,128)(2,1)S(1)} copy(bf16[8,640,2,128]{3,1,2,0:T(8,128)(2,1)} %get-tuple-element.48) | data formatting | bytes 5242880 | tf_op jit(solution)/shard_map/while | solution.py:94
  124.1 1.5 slice.30
  125.7 6.2 %copy.94 = bf16[1,512,2,1024]{3,2,0,1:T(2,128)(2,1)} copy(bf16[1,512,2,1024]{1,3,2,0:T(8,128)(2,1)} %bitcast.153) | data formatting | bytes 4194304 | tf_op jit(solution)/shard_map/reshape | solution.py:99
  131.9 29.2 %all_to_all.40 = bf16[1,512,2,1024]{3,2,0,1:T(2,128)(2,1)S(1)} all-to-all(bf16[1,512,2,1024]{3,2,0,1:T(2,128)(2,1)} %copy.94), channel_id=1, replica_groups=mesh['ctx'=4,'pair'=4,'dp'=2] {'ctx'}, dimensions={1} | all-to-all | bytes 4194304 | tf_op jit(solution)/shard_map/all_to_all | solution.py:100
  161.1 3.1 %reduce_sum.39 = bf16[128,2,1024]{2,1,0:T(2,128)(2,1)S(1)} reduce(bf16[4,128,2,1024]{3,2,1,0:T(2,128)(2,1)S(1)} %bitcast.152, bf16[]{:T(256)} %constant.29.clone.1), dimensions={0}, to_apply=%region_5.6 | reduce | flops 786432 | bytes 2621442 | tf_op jit(solution)/shard_map/reduce_sum | solution.py:101
  164.2 1.9 copy.95
  166.1 4.6 %all-to-all-start.2 = ((bf16[1,128,2,1024]{1,2,0,3:T(2,128)(2,1)}), bf16[1,128,2,1024]{1,2,0,3:T(2,128)(2,1)S(1)}, u32[]{:S(2)}, u32[]{:S(2)}) async-start(bf16[1,128,2,1024]{1,2,0,3:T(2,128)(2,1)} %copy.95), calls=%async_computation.2 | async-start | bytes 1048576 | tf_op jit(solution)/shard_map/all_to_all | solution.py:102
  171.3 1.2 reshape.115
  174.5 9.3 %all-to-all-done.2 = bf16[1,128,2,1024]{1,2,0,3:T(2,128)(2,1)S(1)} async-done(((bf16[1,128,2,1024]{1,2,0,3:T(2,128)(2,1)}), bf16[1,128,2,1024]{1,2,0,3:T(2,128)(2,1)S(1)}, u32[]{:S(2)}, u32[]{:S(2)}) %all-to-all-start.2) | async-done | bytes 524320 | tf_op jit(solution)/shard_map/all_to_all | solution.py:102
  184.5 1.2 copy.98
  (116 shorter events, 33.0 us)
Async XLA Ops:
  7.2 1.4 copy-start
  7.2 59.9 %all-gather.2.cloned.1.call-start = ((), (), s32[]{:S(2)}) async-start(), calls=%async_computation.3 | async-start | bytes 2621440 | tf_op jit(solution)/shard_map/all_gather | solution.py:15
  10.2 22.4 %copy-start.1 = (bf16[1,1,128,2048]{3,2,1,0:T(8,128)(2,1)S(1)}, bf16[1,1,128,2048]{3,2,1,0:T(8,128)(2,1)}, u32[]{:S(2)}) copy-start(bf16[1,1,128,2048]{3,2,1,0:T(8,128)(2,1)} %param.10) | copy-start | bytes 1572868
  10.7 22.2 %copy-start.4 = (bf16[1,1,128,1024]{3,2,1,0:T(8,128)(2,1)S(1)}, bf16[1,1,128,1024]{3,2,1,0:T(8,128)(2,1)}, u32[]{:S(2)}) copy-start(bf16[1,1,128,1024]{3,2,1,0:T(8,128)(2,1)} %param.11) | copy-start | bytes 786436
  10.8 22.4 %copy-start.5 = (bf16[1,1,128,1024]{3,2,1,0:T(8,128)(2,1)S(1)}, bf16[1,1,128,1024]{3,2,1,0:T(8,128)(2,1)}, u32[]{:S(2)}) copy-start(bf16[1,1,128,1024]{3,2,1,0:T(8,128)(2,1)} %param.12) | copy-start | bytes 786436
  31.5 1.8 copy-start.2
  32.6 1.6 copy-start.7
  161.1 9.6 %copy-start.6 = (s32[4]{0:T(128)S(1)}, s32[4]{0:T(128)}, u32[]{:S(2)}) copy-start(s32[4]{0:T(128)} %param.17) | copy-start | bytes 52
  161.1 9.7 %copy-start.3 = (bf16[8,2,128,128]{3,2,1,0:T(8,128)(2,1)S(1)}, bf16[8,2,128,128]{3,2,1,0:T(8,128)(2,1)}, u32[]{:S(2)}) copy-start(bf16[8,2,128,128]{3,2,1,0:T(8,128)(2,1)} %get-tuple-element.47) | copy-start | bytes 1572868
  166.1 17.7 %all-to-all-start.2 = ((bf16[1,128,2,1024]{1,2,0,3:T(2,128)(2,1)}), bf16[1,128,2,1024]{1,2,0,3:T(2,128)(2,1)S(1)}, u32[]{:S(2)}, u32[]{:S(2)}) async-start(bf16[1,128,2,1024]{1,2,0,3:T(2,128)(2,1)} %copy.95), calls=%async_computation.2 | async-start | bytes 1048576 | tf_op jit(solution)/shard_map/all_to_all | solution.py:102
Sparse Core Ops, SparseCore 0:
  32.7 34.2 all-gather.1
where the time goes:
time: 194 us; the launch traced here: 193 us
  blocking collectives  50 us (26%)
  waiting for transfers between devices  41.1 us (21%)
  matrix products  34.8 us (18%)
  local copies, waits for them, and re-layouts  31.2 us (16%)
  other arithmetic  15.5 us (8%)
  between operations  14.9 us (8%)
  starting transfers between devices  4.64 us (2%)
    all_gather x1, waiting for transfers between devices, gather_rows(): return lax.all_gather(kv_part, 'ctx', axis=1, tiled=True)  31.8 us
    all_to_all x1, blocking collectives, shards(): lax.all_to_all(prefix_part, 'ctx', split_axis=1, concat_axis=0, tiled=True)  29.2 us
    all_to_all x1, blocking collectives, pick_prompt(): lax.all_to_all(outgoing, 'pair', split_axis=0, concat_axis=3, tiled=True)  20.7 us
    dot_general x8, matrix products, one_head(): jnp.einsum('jqk,kd->jqd', ds_low, key_rows, preferred_element_type=jnp.fl...  14.4 us
    sub x8, matrix products, one_head(): raised = jnp.exp(scores - row_peak)  11.3 us
    all_to_all x1, waiting for transfers between devices, shards(): lax.all_to_all(ctx_total[None], 'pair', split_axis=3, concat_axis=0, tile...  9.32 us
    dynamic_slice x16, local copies, waits for them, and re-layouts, shards(): lax.map(one_head, (keys_heads, values_heads, query_heads, grad_heads))  7.76 us
    reshape x1, local copies, waits for them, and re-layouts, shards(): jnp.transpose(kv_grads[:, :pre_rows], (1, 2, 0, 3))  6.24 us
  transfers between devices with their start and end apart: 2, of which 2 were waited for; matrix products, arithmetic and copies ran while one was open for 3% of the time, Pallas kernels for 0%

commit v1 on v0

--- a/solution.py
+++ b/solution.py
@@ -11,8 +11,20 @@
 neg_big = -1e30
 
 
+def gather_by_bits(x, axis, dim):
+    ways, here, lap = (lax.axis_size(axis), lax.axis_index(axis), x.shape[dim])
+    line, have = (x, 1)
+    while have < ways:
+        line = jnp.concatenate(
+            [line, lax.ppermute(line, axis, [(d, (d - have) % ways) for d in range(ways)])],
+            axis=dim,
+        )
+        have = 2 * have
+    return jnp.roll(line, here * lap, axis=dim)
+
+
 def gather_rows(kv_part):
-    return lax.all_gather(kv_part, "ctx", axis=1, tiled=True)
+    return gather_by_bits(kv_part, "ctx", 1)
 
 
 def pick_prompt(kv_part, pair_prompt):

time: 194 us -> 178 us (0.918)
  between operations: 14.9 us -> 1.55 us
  waiting for transfers between devices: 41.1 us -> 32.2 us
  starting transfers between devices: 4.64 us -> 8.74 us
  local copies, waits for them, and re-layouts: 31.2 us -> 34.5 us
  blocking collectives: 50 us -> 47.7 us
    all_gather x1 -> x0, waiting for transfers between devices: 31.8 us -> none  [gather_rows(): return lax.all_gather(kv_part, 'ctx', axis=1, tiled=True)]
    ppermute x0 -> x2, waiting for transfers between devices: none -> 26.3 us  [gather_by_bits(): lax.ppermute(line, axis, [(d, (d - have) % ways) for d in range(ways)])]
    unnamed x21 -> x26, local copies, waits for them, and re-layouts: 2.12 us -> 6.18 us
    ppermute x0 -> x2, starting transfers between devices: none -> 4.02 us  [gather_by_bits(): lax.ppermute(line, axis, [(d, (d - have) % ways) for d in range(ways)])]
    all_to_all x1, waiting for transfers between devices: 9.32 us -> 5.84 us  [shards(): lax.all_to_all(ctx_total[None], 'pair', split_axis=3, concat_axis=0, tile...]
    all_to_all x1, blocking collectives: 29.2 us -> 27 us  [shards(): lax.all_to_all(prefix_part, 'ctx', split_axis=1, concat_axis=0, tiled=True)]
  transfers between devices with their start and end apart: 2 -> 3, of which waited for: 2 -> 3; matrix products, arithmetic and copies ran while one was open for 3% -> 5% of each run, Pallas kernels for 0% -> 0%
where the time goes in v1:
time: 178 us; the launch traced here: 177 us
  blocking collectives  47.7 us (27%)
  matrix products  34.8 us (20%)
  local copies, waits for them, and re-layouts  34.5 us (19%)
  waiting for transfers between devices  32.2 us (18%)
  other arithmetic  16.7 us (9%)
  starting transfers between devices  8.74 us (5%)
    all_to_all x1, blocking collectives, shards(): lax.all_to_all(prefix_part, 'ctx', split_axis=1, concat_axis=0, tiled=True)  27 us
    ppermute x2, waiting for transfers between devices, gather_by_bits(): lax.ppermute(line, axis, [(d, (d - have) % ways) for d in range(ways)])  26.3 us
    all_to_all x1, blocking collectives, pick_prompt(): lax.all_to_all(outgoing, 'pair', split_axis=0, concat_axis=3, tiled=True)  20.7 us
    dot_general x8, matrix products, one_head(): jnp.einsum('jqk,kd->jqd', ds_low, key_rows, preferred_element_type=jnp.fl...  14.4 us
    sub x8, matrix products, one_head(): raised = jnp.exp(scores - row_peak)  11.3 us
    dynamic_slice x16, local copies, waits for them, and re-layouts, shards(): lax.map(one_head, (keys_heads, values_heads, query_heads, grad_heads))  7.75 us
    reshape x1, local copies, waits for them, and re-layouts, shards(): jnp.transpose(kv_grads[:, :pre_rows], (1, 2, 0, 3))  6.26 us
    unnamed x26, local copies, waits for them, and re-layouts  6.18 us
  transfers between devices with their start and end apart: 3, of which 3 were waited for; matrix products, arithmetic and copies ran while one was open for 5% of the time, Pallas kernels for 0%

profile of v1, /device:TPU:0, one launch (start us, length us, event | category | flops | bytes accessed | tf_op | source)
XLA Modules:
  0.0 176.5 jit_solution(12557780135112569436)
XLA Ops:
  2.0 1.6 gather_fusion
  4.2 20.7 %all_to_all.39 = bf16[4,128,2,256]{3,2,1,0:T(2,128)(2,1)S(1)} all-to-all(bf16[4,128,2,256]{3,2,1,0:T(2,128)(2,1)S(1)} %broadcast_select_fusion), channel_id=1, replica_groups=mesh['ctx'=4,'pair'=4,'dp'=2] {'pair'}, dimensions={0} | all-to-all | bytes 1048576 | tf_op jit(solution)/shard_map/all_to_all | solution.py:32
  25.4 2.5 %collective-permute-start = (bf16[1,128,2,1024]{1,3,2,0:T(8,128)(2,1)S(1)}, bf16[1,128,2,1024]{1,3,2,0:T(8,128)(2,1)S(1)}, u32[]{:S(2)}, u32[]{:S(2)}) collective-permute-start(bf16[1,128,2,1024]{1,3,2,0:T(8,128)(2,1)S(1)} %bitcast.155), channel_id=1, source_target_pairs={{0,24},{8,0},{16,8},{24,16},{1,25},{9,1},{17,9},{25,17},{2,26},{10... | collective-permute-start | bytes 1572872 | tf_op jit(solution)/shard_map/ppermute | solution.py:19
  27.9 10.1 %collective-permute-done = bf16[1,128,2,1024]{1,3,2,0:T(8,128)(2,1)S(1)} collective-permute-done((bf16[1,128,2,1024]{1,3,2,0:T(8,128)(2,1)S(1)}, bf16[1,128,2,1024]{1,3,2,0:T(8,128)(2,1)S(1)}, u32[]{:S(2)}, u32[]{:S(2)}) %collective-permute-start) | collective-permute-done | bytes 524320 | tf_op jit(solution)/shard_map/ppermute | solution.py:19
  39.1 1.5 collective-permute-start.1
  45.9 16.3 %collective-permute-done.1 = bf16[1,256,2,1024]{1,3,2,0:T(8,128)(2,1)S(1)} collective-permute-done((bf16[1,256,2,1024]{1,3,2,0:T(8,128)(2,1)}, bf16[1,256,2,1024]{1,3,2,0:T(8,128)(2,1)S(1)}, u32[]{:S(2)}, u32[]{:S(2)}) %collective-permute-start.1) | collective-permute-done | bytes 1048608 | tf_op jit(solution)/shard_map/ppermute | solution.py:19
  65.5 50.8 %while.12 = (s32[]{:T(128)}, bf16[8,2,128,128]{3,2,1,0:T(8,128)(2,1)}, bf16[8,640,2,128]{3,1,2,0:T(8,128)(2,1)}, pred[128,640]{1,0:T(8,128)(4,1)S(1)}, bf16[8,2,...) while((s32[]{:T(128)}, ...), condition=%wide.region_4.5_spmd, body=%wide.region_0.4_spmd.sunk | while | flops 254427520 | bytes 6446701 | solution.py:106
  65.5 1.4 fusion.90
  70.0 1.8 %fusion.93 = bf16[8,2,128,128]{3,2,1,0:T(8,128)(2,1)} fusion(bf16[8,2,128,128]{3,2,1,0:T(8,128)(2,1)} %get-tuple-element.180, s32[]{:T(128)} %get-tuple-element.179, bf16[2,128,640]{2,1,0:T(8,128)(2,1)S(1)} %fusion.92, bf16[8,640,128]{1,2,0:T(8,128)(2,1)} %get-tuple-element.193), kind=kOutput, calls=%fused_computation.20.clone.1 | convolution fusion | flops 42008576 | bytes 558080 | tf_op jit(solution)/shard_map/while/body/eval_jaxpr/jqk,kd->jqd/dot_general | solution.py:93
  71.8 1.4 fusion.90
  76.4 1.8 %fusion.93 = bf16[8,2,128,128]{3,2,1,0:T(8,128)(2,1)} fusion(bf16[8,2,128,128]{3,2,1,0:T(8,128)(2,1)} %get-tuple-element.180, s32[]{:T(128)} %get-tuple-element.179, bf16[2,128,640]{2,1,0:T(8,128)(2,1)S(1)} %fusion.92, bf16[8,640,128]{1,2,0:T(8,128)(2,1)} %get-tuple-element.193), kind=kOutput, calls=%fused_computation.20.clone.1 | convolution fusion | flops 42008576 | bytes 558080 | tf_op jit(solution)/shard_map/while/body/eval_jaxpr/jqk,kd->jqd/dot_general | solution.py:93
  78.2 1.4 fusion.90
  82.7 1.8 %fusion.93 = bf16[8,2,128,128]{3,2,1,0:T(8,128)(2,1)} fusion(bf16[8,2,128,128]{3,2,1,0:T(8,128)(2,1)} %get-tuple-element.180, s32[]{:T(128)} %get-tuple-element.179, bf16[2,128,640]{2,1,0:T(8,128)(2,1)S(1)} %fusion.92, bf16[8,640,128]{1,2,0:T(8,128)(2,1)} %get-tuple-element.193), kind=kOutput, calls=%fused_computation.20.clone.1 | convolution fusion | flops 42008576 | bytes 558080 | tf_op jit(solution)/shard_map/while/body/eval_jaxpr/jqk,kd->jqd/dot_general | solution.py:93
  84.5 1.4 fusion.90
  89.1 1.8 %fusion.93 = bf16[8,2,128,128]{3,2,1,0:T(8,128)(2,1)} fusion(bf16[8,2,128,128]{3,2,1,0:T(8,128)(2,1)} %get-tuple-element.180, s32[]{:T(128)} %get-tuple-element.179, bf16[2,128,640]{2,1,0:T(8,128)(2,1)S(1)} %fusion.92, bf16[8,640,128]{1,2,0:T(8,128)(2,1)} %get-tuple-element.193), kind=kOutput, calls=%fused_computation.20.clone.1 | convolution fusion | flops 42008576 | bytes 558080 | tf_op jit(solution)/shard_map/while/body/eval_jaxpr/jqk,kd->jqd/dot_general | solution.py:93
  90.9 1.4 fusion.90
  95.4 1.8 %fusion.93 = bf16[8,2,128,128]{3,2,1,0:T(8,128)(2,1)} fusion(bf16[8,2,128,128]{3,2,1,0:T(8,128)(2,1)} %get-tuple-element.180, s32[]{:T(128)} %get-tuple-element.179, bf16[2,128,640]{2,1,0:T(8,128)(2,1)S(1)} %fusion.92, bf16[8,640,128]{1,2,0:T(8,128)(2,1)} %get-tuple-element.193), kind=kOutput, calls=%fused_computation.20.clone.1 | convolution fusion | flops 42008576 | bytes 558080 | tf_op jit(solution)/shard_map/while/body/eval_jaxpr/jqk,kd->jqd/dot_general | solution.py:93
  97.2 1.4 fusion.90
  101.8 1.8 %fusion.93 = bf16[8,2,128,128]{3,2,1,0:T(8,128)(2,1)} fusion(bf16[8,2,128,128]{3,2,1,0:T(8,128)(2,1)} %get-tuple-element.180, s32[]{:T(128)} %get-tuple-element.179, bf16[2,128,640]{2,1,0:T(8,128)(2,1)S(1)} %fusion.92, bf16[8,640,128]{1,2,0:T(8,128)(2,1)} %get-tuple-element.193), kind=kOutput, calls=%fused_computation.20.clone.1 | convolution fusion | flops 42008576 | bytes 558080 | tf_op jit(solution)/shard_map/while/body/eval_jaxpr/jqk,kd->jqd/dot_general | solution.py:93
  103.6 1.4 fusion.90
  108.2 1.8 %fusion.93 = bf16[8,2,128,128]{3,2,1,0:T(8,128)(2,1)} fusion(bf16[8,2,128,128]{3,2,1,0:T(8,128)(2,1)} %get-tuple-element.180, s32[]{:T(128)} %get-tuple-element.179, bf16[2,128,640]{2,1,0:T(8,128)(2,1)S(1)} %fusion.92, bf16[8,640,128]{1,2,0:T(8,128)(2,1)} %get-tuple-element.193), kind=kOutput, calls=%fused_computation.20.clone.1 | convolution fusion | flops 42008576 | bytes 558080 | tf_op jit(solution)/shard_map/while/body/eval_jaxpr/jqk,kd->jqd/dot_general | solution.py:93
  109.9 1.4 fusion.90
  114.5 1.8 %fusion.93 = bf16[8,2,128,128]{3,2,1,0:T(8,128)(2,1)} fusion(bf16[8,2,128,128]{3,2,1,0:T(8,128)(2,1)} %get-tuple-element.180, s32[]{:T(128)} %get-tuple-element.179, bf16[2,128,640]{2,1,0:T(8,128)(2,1)S(1)} %fusion.92, bf16[8,640,128]{1,2,0:T(8,128)(2,1)} %get-tuple-element.193), kind=kOutput, calls=%fused_computation.20.clone.1 | convolution fusion | flops 42008576 | bytes 558080 | tf_op jit(solution)/shard_map/while/body/eval_jaxpr/jqk,kd->jqd/dot_general | solution.py:93
  116.3 3.2 %copy.93 = bf16[8,640,2,128]{1,3,0,2:T(8,128)(2,1)S(1)} copy(bf16[8,640,2,128]{3,1,2,0:T(8,128)(2,1)} %get-tuple-element.48) | data formatting | bytes 5242880 | tf_op jit(solution)/shard_map/while | solution.py:106
  119.5 1.5 slice.30
  121.0 6.3 %copy.94 = bf16[1,512,2,1024]{3,2,0,1:T(2,128)(2,1)} copy(bf16[1,512,2,1024]{1,3,2,0:T(8,128)(2,1)} %bitcast.154) | data formatting | bytes 4194304 | tf_op jit(solution)/shard_map/reshape | solution.py:111
  127.2 27.0 %all_to_all.40 = bf16[1,512,2,1024]{3,2,0,1:T(2,128)(2,1)S(1)} all-to-all(bf16[1,512,2,1024]{3,2,0,1:T(2,128)(2,1)} %copy.94), channel_id=1, replica_groups=mesh['ctx'=4,'pair'=4,'dp'=2] {'ctx'}, dimensions={1} | all-to-all | bytes 4194304 | tf_op jit(solution)/shard_map/all_to_all | solution.py:112
  154.2 3.1 %reduce_sum.39 = bf16[128,2,1024]{2,1,0:T(2,128)(2,1)S(1)} reduce(bf16[4,128,2,1024]{3,2,1,0:T(2,128)(2,1)S(1)} %bitcast.153, bf16[]{:T(256)} %constant.68.clone.1), dimensions={0}, to_apply=%region_5.6 | reduce | flops 786432 | bytes 2621442 | tf_op jit(solution)/shard_map/reduce_sum | solution.py:113
  157.3 1.9 %copy.95 = bf16[1,128,2,1024]{1,2,0,3:T(2,128)(2,1)} copy(bf16[1,128,2,1024]{3,2,1,0:T(2,128)(2,1)S(1)} %bitcast.164) | data formatting | bytes 1048576 | tf_op jit(solution)/shard_map/broadcast_in_dim | solution.py:114
  159.2 4.7 %all-to-all-start.2 = ((bf16[1,128,2,1024]{1,2,0,3:T(2,128)(2,1)}), bf16[1,128,2,1024]{1,2,0,3:T(2,128)(2,1)S(1)}, u32[]{:S(2)}, u32[]{:S(2)}) async-start(bf16[1,128,2,1024]{1,2,0,3:T(2,128)(2,1)} %copy.95), calls=%async_computation.2 | async-start | bytes 1048576 | tf_op jit(solution)/shard_map/all_to_all | solution.py:114
  164.0 1.6 copy.91
  168.7 5.8 %all-to-all-done.2 = bf16[1,128,2,1024]{1,2,0,3:T(2,128)(2,1)S(1)} async-done(((bf16[1,128,2,1024]{1,2,0,3:T(2,128)(2,1)}), bf16[1,128,2,1024]{1,2,0,3:T(2,128)(2,1)S(1)}, u32[]{:S(2)}, u32[]{:S(2)}) %all-to-all-start.2) | async-done | bytes 524320 | tf_op jit(solution)/shard_map/all_to_all | solution.py:114
  (125 shorter events, 41.1 us)
Async XLA Ops:
  0.6 1.4 copy-start
  0.6 27.3 %copy-start.7 = (s32[1,1,4]{2,1,0:T(1,128)S(1)}, s32[1,1,4]{2,1,0:T(1,128)}, u32[]{:S(2)}) copy-start(s32[1,1,4]{2,1,0:T(1,128)} %param.15) | copy-start | bytes 52
  3.6 37.1 %copy-start.4 = (bf16[1,1,128,1024]{3,2,1,0:T(8,128)(2,1)S(1)}, bf16[1,1,128,1024]{3,2,1,0:T(8,128)(2,1)}, u32[]{:S(2)}) copy-start(bf16[1,1,128,1024]{3,2,1,0:T(8,128)(2,1)} %param.11) | copy-start | bytes 786436
  4.2 37.4 %copy-start.5 = (bf16[1,1,128,1024]{3,2,1,0:T(8,128)(2,1)S(1)}, bf16[1,1,128,1024]{3,2,1,0:T(8,128)(2,1)}, u32[]{:S(2)}) copy-start(bf16[1,1,128,1024]{3,2,1,0:T(8,128)(2,1)} %param.12) | copy-start | bytes 786436
  4.2 38.2 %copy-start.3 = (bf16[1,1,128,2048]{3,2,1,0:T(8,128)(2,1)S(1)}, bf16[1,1,128,2048]{3,2,1,0:T(8,128)(2,1)}, u32[]{:S(2)}) copy-start(bf16[1,1,128,2048]{3,2,1,0:T(8,128)(2,1)} %param.13) | copy-start | bytes 1572868
  25.4 12.6 %collective-permute-start = (bf16[1,128,2,1024]{1,3,2,0:T(8,128)(2,1)S(1)}, bf16[1,128,2,1024]{1,3,2,0:T(8,128)(2,1)S(1)}, u32[]{:S(2)}, u32[]{:S(2)}) collective-permute-start(bf16[1,128,2,1024]{1,3,2,0:T(8,128)(2,1)S(1)} %bitcast.155), channel_id=1, source_target_pairs={{0,24},{8,0},{16,8},{24,16},{1,25},{9,1},{17,9},{25,17},{2,26},{10... | collective-permute-start | bytes 1572872 | tf_op jit(solution)/shard_map/ppermute | solution.py:19
  39.1 23.1 %collective-permute-start.1 = (bf16[1,256,2,1024]{1,3,2,0:T(8,128)(2,1)}, bf16[1,256,2,1024]{1,3,2,0:T(8,128)(2,1)S(1)}, u32[]{:S(2)}, u32[]{:S(2)}) collective-permute-start(bf16[1,256,2,1024]{1,3,2,0:T(8,128)(2,1)} %pad_maximum_fusion), channel_id=1, source_target_pairs={{0,16},{8,24},{16,0},{24,8},{1,17},{9,25},{17,1},{25,9},{2,18},{10... | collective-permute-start | bytes 3145736 | tf_op jit(solution)/shard_map/ppermute | solution.py:19
  63.1 1.0 copy-start.1
  63.1 1.0 copy-start.2
  154.2 9.7 %copy-start.6 = (s32[4]{0:T(128)S(1)}, s32[4]{0:T(128)}, u32[]{:S(2)}) copy-start(s32[4]{0:T(128)} %param.17) | copy-start | bytes 52
  159.2 15.3 %all-to-all-start.2 = ((bf16[1,128,2,1024]{1,2,0,3:T(2,128)(2,1)}), bf16[1,128,2,1024]{1,2,0,3:T(2,128)(2,1)S(1)}, u32[]{:S(2)}, u32[]{:S(2)}) async-start(bf16[1,128,2,1024]{1,2,0,3:T(2,128)(2,1)} %copy.95), calls=%async_computation.2 | async-start | bytes 1048576 | tf_op jit(solution)/shard_map/all_to_all | solution.py:114
